TPU v7x, 32 devices: a whole 2x2x4 slice. The times are simulated.
32 devices in a mesh: ctx: 16 (over z, y, x), tp: 2 (over core).
Axes of the slice: x: 2, y: 2, z: 4, core: 2. Of those that a mesh axis runs over, the one named last changes fastest.
Arguments:
- x_act: bfloat16 [4096, 8192], P('ctx', 'tp'), may hold values from -0.119628906 to 0.119628906
- b_proj: bfloat16 [4096, 128], P('ctx'), may hold values from -0.5 to 0.5
- c_proj: bfloat16 [4096, 128], P('ctx'), may hold values from -0.5 to 0.5
- dt_raw: bfloat16 [4096, 128], P('ctx', 'tp'), may hold values from -3 to 3
- a_log: float32 [128], P('tp'), may hold values from -12 to -2
- d_skip: float32 [128], P('tp'), may hold values from 0.5 to 2
- grad_out: bfloat16 [4096, 8192], P('ctx', 'tp'), may hold values from -6 to 6
Outputs:
- grad_x: bfloat16 [4096, 8192], P('ctx', 'tp')
- grad_b: float32 [4096, 128], P('ctx')
- grad_c: float32 [4096, 128], P('ctx')
- grad_dt: bfloat16 [4096, 128], P('ctx', 'tp')
All inputs are finite; a program needn't handle non-finite values.
Results may differ from a plain program's by a relative error of at most 0.001.
Values may be sent and summed in bfloat16 or wider, within the bound.
No kernel may reach another device: no remote copies, remote signals or barrier semaphores. Data moves between devices by JAX's collectives and lax.ppermute only.
A program may use at most 192 MiB of HBM per device.

v0:
```python
from functools import partial
import jax
import jax.numpy as jnp
from jax import lax
from jax.sharding import PartitionSpec as P

BLOCK = 256
precise = lax.Precision.HIGH


def head_forward(x_head, b_rows, c_rows, raw_step, log_rate, skip_gain, start_state, block_len):
    length, head_width = x_head.shape
    blocks = length // block_len
    step_size = jax.nn.softplus(raw_step)
    decay_rates = -jnp.exp(log_rate) * step_size
    row_index = lax.broadcasted_iota(jnp.int32, (block_len, block_len), 0)
    col_index = lax.broadcasted_iota(jnp.int32, (block_len, block_len), 1)
    lower_mask = row_index >= col_index
    running = jnp.dot(
        decay_rates.reshape(blocks, block_len), lower_mask.astype(jnp.float32).T, precision=precise
    )
    between = jnp.where(lower_mask[None], running[:, :, None] - running[:, None, :], -1e30)
    x_blocks = x_head.reshape(blocks, block_len, head_width)
    b_blocks = b_rows.reshape(blocks, block_len, -1)
    c_blocks = c_rows.reshape(blocks, block_len, -1)
    s_blocks = step_size.reshape(blocks, block_len)
    scores = (
        jnp.einsum("kin,kjn->kij", c_blocks, b_blocks, precision=precise)
        * jnp.exp(between)
        * s_blocks[:, None, :]
    )
    output = jnp.einsum("kij,kjp->kip", scores, x_blocks, precision=precise)
    closing = running[:, -1]
    weighted = (jnp.exp(closing[:, None] - running) * s_blocks)[:, :, None] * x_blocks
    states = jnp.einsum("kjp,kjn->kpn", weighted, b_blocks, precision=precise)
    block_rows = lax.broadcasted_iota(jnp.int32, (blocks, blocks), 0)
    block_cols = lax.broadcasted_iota(jnp.int32, (blocks, blocks), 1)
    through = jnp.dot((block_rows >= block_cols).astype(jnp.float32), closing, precision=precise)
    before = through - closing
    carry_weight = jnp.exp(
        jnp.where(block_rows > block_cols, before[:, None] - through[None, :], -1e30)
    )
    entering = (
        jnp.einsum("kj,jpn->kpn", carry_weight, states, precision=precise)
        + jnp.exp(before)[:, None, None] * start_state[None]
    )
    reading = jnp.exp(running)[:, :, None] * c_blocks
    output = output + jnp.einsum("kin,kpn->kip", reading, entering, precision=precise)
    output = output.reshape(length, head_width) + skip_gain * x_head
    final_state = (
        jnp.einsum("j,jpn->pn", jnp.exp(through[-1] - through), states, precision=precise)
        + jnp.exp(through[-1]) * start_state
    )
    return (output, final_state)


N_CHUNKS = 1


def chunk_backward(x_seq, g_seq, raw_seq, b_rows, c_rows, rate, gain):
    length = x_seq.shape[0]
    heads = raw_seq.shape[1]
    head_width = x_seq.shape[1] // heads
    runner = partial(head_forward, block_len=BLOCK)
    mapped = jax.vmap(runner, in_axes=(0, None, None, 0, 0, 0, 0))
    x_heads = x_seq.astype(jnp.float32).reshape(length, heads, head_width).transpose(1, 0, 2)
    g_heads = g_seq.astype(jnp.float32).reshape(length, heads, head_width).transpose(1, 0, 2)
    raw_heads = raw_seq.astype(jnp.float32).T
    anchor = jnp.zeros((heads, head_width, b_rows.shape[1]), jnp.float32)

    def forward(x_val, b_val, c_val, raw_val):
        return mapped(x_val, b_val, c_val, raw_val, rate, gain, anchor)[0]

    _, pullback = jax.vjp(forward, x_heads, b_rows, c_rows, raw_heads)
    grad_xh, grad_b_all, grad_c_all, grad_raw = pullback(g_heads)
    x_back = grad_xh.transpose(1, 0, 2).reshape(length, heads * head_width).astype(jnp.bfloat16)
    raw_back = grad_raw.T
    return (x_back, raw_back, grad_b_all, grad_c_all)


def gather_ctx(block, owners, me):
    if owners & owners - 1:
        return lax.all_gather(block, "ctx", axis=0, tiled=True)
    have = block
    step = 1
    while step < owners:
        theirs = lax.ppermute(have, "ctx", [(k, k ^ step) for k in range(owners)])
        upper = me // step % 2 == 1
        have = jnp.where(upper, jnp.concatenate([theirs, have]), jnp.concatenate([have, theirs]))
        step *= 2
    return have


def local(x_act, b_proj, c_proj, dt_raw, a_log, d_skip, grad_out):
    rows = x_act.shape[0]
    heads_here = dt_raw.shape[1]
    head_width = x_act.shape[1] // heads_here
    state = b_proj.shape[1]
    owners = lax.axis_size("ctx")
    per_owner = heads_here // owners
    chunks = N_CHUNKS if per_owner % N_CHUNKS == 0 else 1
    per_chunk = per_owner // chunks
    me = lax.axis_index("ctx")
    half = lax.axis_index("tp")
    own_seq = gather_ctx(jnp.where(half == 0, b_proj, c_proj), owners, me)
    other_seq = lax.ppermute(own_seq, "tp", [(0, 1), (1, 0)])
    b_rows = jnp.where(half == 0, own_seq, other_seq).astype(jnp.float32)
    c_rows = jnp.where(half == 0, other_seq, own_seq).astype(jnp.float32)
    first_head = me * per_owner
    rate_own = lax.dynamic_slice_in_dim(a_log, first_head, per_owner)
    gain_own = lax.dynamic_slice_in_dim(d_skip, first_head, per_owner)
    x4 = x_act.reshape(rows, owners, per_owner, head_width)
    g4 = grad_out.reshape(rows, owners, per_owner, head_width)
    r3 = dt_raw.reshape(rows, owners, per_owner)
    x_parts, raw_parts = ([], [])
    grad_b_all = None
    grad_c_all = None
    for c in range(chunks):
        sl = slice(c * per_chunk, (c + 1) * per_chunk)
        width = per_chunk * head_width
        x_in = x4[:, :, sl, :].reshape(rows, owners, width)
        g_in = g4[:, :, sl, :].reshape(rows, owners, width)
        if c == 0:
            g_in, _ = lax.optimization_barrier((g_in, own_seq))
        x_seq = lax.all_to_all(x_in, "ctx", split_axis=1, concat_axis=0, tiled=True).reshape(
            rows * owners, width
        )
        g_seq = lax.all_to_all(g_in, "ctx", split_axis=1, concat_axis=0, tiled=True).reshape(
            rows * owners, width
        )
        raw_seq = lax.all_to_all(
            r3[:, :, sl], "ctx", split_axis=1, concat_axis=0, tiled=True
        ).reshape(rows * owners, per_chunk)
        x_back, raw_back, gb, gc = chunk_backward(
            x_seq, g_seq, raw_seq, b_rows, c_rows, rate_own[sl], gain_own[sl]
        )
        x_parts.append(
            lax.all_to_all(x_back, "ctx", split_axis=0, concat_axis=1, tiled=True).reshape(
                rows, owners, 1, width
            )
        )
        raw_parts.append(raw_back)
        grad_b_all = gb if grad_b_all is None else grad_b_all + gb
        grad_c_all = gc if grad_c_all is None else grad_c_all + gc
    grad_x = jnp.concatenate(x_parts, axis=2).reshape(rows, owners * per_owner * head_width)
    raw_all = jnp.concatenate(raw_parts, axis=1)
    is_first = half == 0
    send = jnp.where(is_first, grad_c_all, grad_b_all)
    keep = jnp.where(is_first, grad_b_all, grad_c_all)
    mine = keep + lax.ppermute(send, "tp", [(0, 1), (1, 0)])
    steps_back = raw_all.reshape(owners, rows, per_owner).transpose(0, 2, 1)
    extra = per_owner * rows // state
    if extra * state == per_owner * rows:
        packed = jnp.concatenate(
            [mine.reshape(owners, rows, state), steps_back.reshape(owners, extra, state)], axis=1
        )
        parts = lax.all_to_all(packed, "ctx", split_axis=0, concat_axis=0, tiled=True)
        mine = parts[:, :rows, :].sum(axis=0)
        got_dt = parts[:, rows:, :].reshape(owners, per_owner, rows)
    else:
        parts = lax.all_to_all(
            mine.reshape(owners, rows, state), "ctx", split_axis=0, concat_axis=0, tiled=True
        )
        mine = parts.sum(axis=0)
        got_dt = lax.all_to_all(steps_back, "ctx", split_axis=0, concat_axis=0, tiled=True)
    grad_dt = got_dt.transpose(2, 0, 1).reshape(rows, heads_here).astype(jnp.bfloat16)
    other = lax.ppermute(mine, "tp", [(0, 1), (1, 0)])
    grad_b = jnp.where(is_first, mine, other)
    grad_c = jnp.where(is_first, other, mine)
    return (grad_x, grad_b, grad_c, grad_dt)


def solution(mesh):
    in_specs = (
        P("ctx", "tp"),
        P("ctx", None),
        P("ctx", None),
        P("ctx", "tp"),
        P("tp"),
        P("tp"),
        P("ctx", "tp"),
    )
    out_specs = (P("ctx", "tp"), P("ctx", None), P("ctx", None), P("ctx", "tp"))
    return jax.shard_map(local, mesh=mesh, in_specs=in_specs, out_specs=out_specs, check_vma=False)
```

profile of v0, /device:TPU:12, one launch (start us, length us, event | category | flops | bytes accessed | tf_op | source)
XLA Modules:
  0.0 329.9 jit_solution(7301412444082762005)
XLA Ops:
  0.6 1.4 reshape.136
  2.0 7.2 %all-to-all-start.1 = ((bf16[256,16,4]{0,2,1:T(4,128)(2,1)}), bf16[256,16,4]{0,2,1:T(4,128)(2,1)S(1)}, u32[]{:S(2)}, u32[]{:S(2)}) async-start(bf16[256,16,4]{0,2,1:T(4,128)(2,1)} %reshape.136), calls=%async_computation.1 | async-start | bytes 65536 | tf_op jit(solution)/shard_map/all_to_all | solution.py:131
  9.2 4.1 %copy.83 = bf16[256,4096]{0,1:T(8,128)(2,1)} copy(bf16[256,4096]{1,0:T(8,128)(2,1)} %param.7) | data formatting | bytes 4194304 | tf_op args[0]
  13.3 1.2 all-to-all-done.1
  14.4 5.9 %all-to-all-start.3 = ((bf16[256,16,256]{0,2,1:T(8,128)(2,1)}), bf16[256,16,256]{0,2,1:T(8,128)(2,1)S(1)}, u32[]{:S(2)}, u32[]{:S(2)}) async-start(bf16[256,16,256]{0,2,1:T(8,128)(2,1)} %bitcast.189), calls=%async_computation.3 | async-start | bytes 4194304 | tf_op jit(solution)/shard_map/all_to_all | solution.py:125
  20.4 1.5 collective-permute-start
  21.9 6.7 %collective-permute-done = bf16[256,128]{1,0:T(8,128)(2,1)S(1)} collective-permute-done((bf16[256,128]{1,0:T(8,128)(2,1)S(1)}, bf16[256,128]{1,0:T(8,128)(2,1)S(1)}, u32[]{:S(2)}, u32[]{:S(2)}) %collective-permute-start) | collective-permute-done | bytes 65568 | tf_op jit(solution)/shard_map/ppermute | solution.py:87
  28.7 0.8 collective-permute-start.1
  29.5 4.9 %collective-permute-done.1 = bf16[512,128]{1,0:T(8,128)(2,1)S(1)} collective-permute-done((bf16[512,128]{1,0:T(8,128)(2,1)S(1)}, bf16[512,128]{1,0:T(8,128)(2,1)S(1)}, u32[]{:S(2)}, u32[]{:S(2)}) %collective-permute-start.1) | collective-permute-done | bytes 131104 | tf_op jit(solution)/shard_map/ppermute | solution.py:87
  34.5 2.6 collective-permute-start.2
  37.2 22.8 %collective-permute-done.2 = bf16[1024,128]{1,0:T(8,128)(2,1)S(1)} collective-permute-done((bf16[1024,128]{1,0:T(8,128)(2,1)S(1)}, bf16[1024,128]{1,0:T(8,128)(2,1)S(1)}, u32[]{:S(2)}, u32[]{:S(2)}) %collective-permute-start.2) | collective-permute-done | bytes 262176 | tf_op jit(solution)/shard_map/ppermute | solution.py:87
  60.0 0.1 maximum_select_fusion.1
  60.2 3.5 %collective-permute-start.3 = (bf16[2048,128]{1,0:T(8,128)(2,1)S(1)}, bf16[2048,128]{1,0:T(8,128)(2,1)}, u32[]{:S(2)}, u32[]{:S(2)}) collective-permute-start(bf16[2048,128]{1,0:T(8,128)(2,1)S(1)} %maximum_select_fusion.1), channel_id=1, source_target_pairs={{0,16},{2,18},{4,20},{6,22},{8,24},{10,26},{12,28},{14,30},{16,0},... | collective-permute-start | bytes 1572872 | tf_op jit(solution)/shard_map/ppermute | solution.py:87
  63.7 4.1 %copy.70 = bf16[256,4096]{0,1:T(8,128)(2,1)} copy(bf16[256,4096]{1,0:T(8,128)(2,1)} %param.13) | data formatting | bytes 4194304 | tf_op args[6]
  67.8 20.4 %collective-permute-done.3 = bf16[2048,128]{1,0:T(8,128)(2,1)} collective-permute-done((bf16[2048,128]{1,0:T(8,128)(2,1)S(1)}, bf16[2048,128]{1,0:T(8,128)(2,1)}, u32[]{:S(2)}, u32[]{:S(2)}) %collective-permute-start.3) | collective-permute-done | bytes 524320 | tf_op jit(solution)/shard_map/ppermute | solution.py:87
  88.2 1.8 maximum_select_fusion
  90.1 8.1 %all-to-all-start = ((bf16[256,16,256]{0,2,1:T(8,128)(2,1)}), bf16[256,16,256]{0,2,1:T(8,128)(2,1)}, u32[]{:S(2)}, u32[]{:S(2)}) async-start(bf16[256,16,256]{0,2,1:T(8,128)(2,1)} %bitcast.190), calls=%async_computation | async-start | bytes 4194304 | tf_op jit(solution)/shard_map/all_to_all | solution.py:128
  98.5 0.6 copy.227
  99.2 0.2 fusion.111
  99.4 0.2 slice_reduce_fusion.1
  99.6 0.7 exponential_multiply_fusion
  100.3 0.8 collective-permute-done.4
  101.1 0.1 broadcast_select_fusion.3
  101.2 1.7 copy.73
  102.9 2.8 fusion.112
  105.7 2.5 copy.84
  108.2 2.9 reshape.142
  111.1 33.6 %all-to-all-done = bf16[256,16,256]{0,2,1:T(8,128)(2,1)} async-done(((bf16[256,16,256]{0,2,1:T(8,128)(2,1)}), bf16[256,16,256]{0,2,1:T(8,128)(2,1)}, u32[]{:S(2)}, u32[]{:S(2)}) %all-to-all-start) | async-done | bytes 2097184 | tf_op jit(solution)/shard_map/all_to_all | solution.py:128
  144.7 4.1 %copy.71 = bf16[16,256,1,256]{1,0,3,2:T(8,128)(2,1)} copy(bf16[16,256,1,256]{1,3,0,2:T(8,128)(2,1)} %bitcast.2) | data formatting | bytes 4194304 | tf_op jit(solution)/shard_map/all_to_all | solution.py:128
  148.8 4.2 %reshape.135 = bf16[4096,4,64]{0,2,1:T(8,128)(2,1)} reshape(bf16[16,256,1,256]{1,0,3,2:T(8,128)(2,1)} %copy.71) | data formatting | bytes 4194304 | tf_op jit(solution)/shard_map/reshape | solution.py:128
  153.0 5.9 %multiply_reduce_fusion.4 = (f32[4,16]{1,0:T(4,128)}, f32[4,16,64,128]{3,2,1,0:T(8,128)S(1)}) fusion(f32[16,256,128]{1,2,0:T(8,128)} %copy.73, f32[4,16,256]{2,1,0:T(8,128)S(1)} %get-tuple-element.36, bf16[4,8,16,8,256]{4,3,2,1,0:T(8,128)(2,1)} %bitcast.179), kind=kOutput, calls=%fused_computation.42 | convolution fusion | flops 808452032 | bytes 6357248 | tf_op jit(solution)/shard_map/transpose(jvp(vmap(kin,kpn->kip)))/dot_general | solution.py:48
  158.9 2.0 fusion.44
  160.9 4.0 %fusion.10 = (f32[4,16,256]{2,0,1:T(4,128)S(1)}, f32[16,4,64,256]{3,2,1,0:T(8,128)}) fusion(bf16[4,8,16,8,256]{4,3,2,1,0:T(8,128)(2,1)S(1)} %bitcast.171, bf16[16,256,128,1]{2,1,3,0:T(8,128)(2,1)S(1)} %bitcast.176, f32[16,4,64,128]{3,0,2,1:T(8,128)S(1)} %fusion.44), kind=kOutput, calls=%fused_computation.18 | convolution fusion | flops 808435712 | bytes 9502720 | tf_op jit(solution)/shard_map/transpose(jvp(vmap(kjp,kjn->kpn)))/dot_general | solution.py:35
  164.9 16.5 %fusion.5 = (f32[4,16,256]{2,1,0:T(8,128)}, f32[4,16,256]{2,1,0:T(8,128)}, f32[4,16,256]{2,1,0:T(8,128)S(1)}, f32[16,256,256]{2,1,0:T(8,128)}, f32[4,16,256,256]{3,2,1,0:T(8,128)}) fusion(f32[4,16,256]{2,1,0:T(8,128)S(1)} %bitcast.204, f32[4,16,256]{2,1,0:T(8,128)S(1)} %get-tuple-element.37, f32[16,256,256]{2,1,0:T(8,128)S(1)} %copy-done.12, ...), kind=kOutput, calls=%fused_computation.9 | convolution fusion | flops 594493440 | bytes 29753344 | tf_op jit(solution)/shard_map/transpose(jvp(vmap(kij,kjp->kip)))/dot_general | solution.py:32
  181.5 0.8 fusion.109
  182.3 5.2 %fusion.9 = f32[16,256,128,1]{2,1,3,0:T(8,128)} fusion(f32[4,16,256]{2,0,1:T(4,128)S(1)} %copy.72, f32[16,4,64,128]{3,0,2,1:T(8,128)S(1)} %fusion.44, bf16[4,8,16,8,256]{4,3,2,1,0:T(8,128)(2,1)S(1)} %bitcast.173), kind=kOutput, calls=%fused_computation.17 | convolution fusion | flops 807403520 | bytes 6356992 | tf_op jit(solution)/shard_map/transpose(jvp(vmap(kjp,kjn->kpn)))/dot_general | solution.py:35
  187.5 1.3 fusion.8
  188.8 1.3 copy-done
  190.2 2.0 fusion.47
  192.2 5.1 %multiply_reduce_fusion.3 = (f32[16,256,128]{1,2,0:T(8,128)}, f32[4,16,256]{2,1,0:T(8,128)}) fusion(f32[4,16,256]{2,1,0:T(8,128)S(1)} %copy-done.18, f32[16,256,128]{1,2,0:T(8,128)S(1)} %copy-done.13, f32[4,16,64,128]{3,1,2,0:T(8,128)S(1)} %fusion.47, bf16[4,8,16,8,256]{4,3,2,1,0:T(8,128)(2,1)S(1)} %bitcast.181), kind=kOutput, calls=%fused_computation.11 | convolution fusion | flops 813154304 | bytes 8519680 | tf_op jit(solution)/shard_map/transpose(jvp(vmap(kin,kpn->kip)))/dot_general | solution.py:48
  197.3 2.1 copy.93
  199.4 3.7 %convolution_add_fusion = f32[16,256,128]{2,1,0:T(8,128)S(1)} fusion(f32[16,256,128]{2,1,0:T(8,128)S(1)} %copy.93, f32[16,256,256]{2,1,0:T(8,128)} %get-tuple-element.17, bf16[16,256,128]{2,1,0:T(8,128)(2,1)S(1)} %bitcast.178), kind=kOutput, calls=%fused_computation.57 | convolution fusion | flops 805830656 | bytes 9437184 | tf_op jit(solution)/shard_map/transpose(jvp(vmap(kin,kjn->kij)))/dot_general | solution.py:28
  203.1 0.7 copy-done.11
  203.8 3.8 %broadcast_select_fusion.1 = (f32[16,256,128]{2,1,0:T(8,128)S(1)}, f32[16,256,128]{2,1,0:T(8,128)}) fusion(f32[16,256,128]{2,1,0:T(8,128)S(1)} %convolution_add_fusion, pred[]{:T(512)S(6)} %eq.35, f32[16,256,256]{2,1,0:T(8,128)S(1)} %copy-done.4, bf16[16,256,128]{2,1,0:T(8,128)(2,1)S(1)} %bitcast.186, f32[16,256,128,1]{2,1,3,0:T(8,128)S(1)} %copy-done.11), kind=kOutput, calls=%fused_computation.72 | convolution fusion | flops 806879232 | bytes 13631489 | tf_op jit(solution)/shard_map/transpose(jvp(vmap(kin,kjn->kij)))/dot_general | solution.py:28
  207.7 3.7 %fusion.110 = (f32[4,16]{1,0:T(4,128)S(1)}, f32[4,16]{1,0:T(4,128)S(1)}) fusion(f32[4,16]{1,0:T(4,128)S(1)} %get-tuple-element.38, f32[4,16]{1,0:T(4,128)S(1)} %get-tuple-element.23, f32[16,4,64,128]{3,2,1,0:T(8,128)S(1)} %copy-done.1, f32[4,16,64,128]{3,2,1,0:T(8,128)S(1)} %copy-done.10, pred[16,16]{1,0:T(8,128)(4,1)S(1)} %iota_compare_fusion.6), kind=kOutput, calls=%fused_computation.136 | convolution fusion | flops 50337664 | bytes 4195584 | tf_op jit(solution)/shard_map/transpose(jvp(vmap(kj,jpn->kpn)))/dot_general | solution.py:44
  211.4 0.1 fusion.71
  211.7 0.2 convolution_bitcast_fusion
  212.0 0.1 fusion.77
  212.2 1.8 bitcast_add_fusion.1
  214.0 1.5 pad_maximum_fusion
  215.6 5.7 %all-to-all-start.4 = ((f32[16,264,128]{2,1,0:T(8,128)}), f32[16,264,128]{2,1,0:T(8,128)}, u32[]{:S(2)}, u32[]{:S(2)}) async-start(f32[16,264,128]{2,1,0:T(8,128)} %pad_maximum_fusion), calls=%async_computation.4 | async-start | bytes 4325376 | tf_op jit(solution)/shard_map/all_to_all | solution.py:157
  221.3 9.0 %fusion.12 = f32[16,4,8,8,256]{4,3,2,1,0:T(8,128)S(1)} fusion(f32[16,4,64,256]{3,2,1,0:T(8,128)} %get-tuple-element.40, f32[4,16,256]{2,0,1:T(4,128)S(1)} %copy.72, bf16[4,8,16,8,256]{4,3,2,1,0:T(8,128)(2,1)S(1)} %bitcast.182, f32[4,16,256,256]{3,2,1,0:T(8,128)} %get-tuple-element.24), kind=kOutput, calls=%fused_computation.21 | convolution fusion | flops 1612709888 | bytes 27328512 | tf_op jit(solution)/shard_map/transpose(jvp(vmap(kij,kjp->kip)))/dot_general | solution.py:32
  230.3 0.6 copy.117
  230.9 0.8 fusion.13
  231.7 0.6 copy.120
  232.3 2.0 copy.82
  234.3 36.7 %all-to-all-done.4 = f32[16,264,128]{2,1,0:T(8,128)} async-done(((f32[16,264,128]{2,1,0:T(8,128)}), f32[16,264,128]{2,1,0:T(8,128)}, u32[]{:S(2)}, u32[]{:S(2)}) %all-to-all-start.4) | async-done | bytes 2162720 | tf_op jit(solution)/shard_map/all_to_all | solution.py:157
  271.0 5.7 %all-to-all-start.2 = ((bf16[16,256,256]{1,2,0:T(8,128)(2,1)}), bf16[16,256,256]{1,2,0:T(8,128)(2,1)S(1)}, u32[]{:S(2)}, u32[]{:S(2)}) async-start(bf16[16,256,256]{1,2,0:T(8,128)(2,1)} %copy.82), calls=%async_computation.2 | async-start | bytes 4194304 | tf_op jit(solution)/shard_map/all_to_all | solution.py:138
  276.7 1.7 slice_reduce_fusion
  278.5 46.1 %all-to-all-done.2 = bf16[16,256,256]{1,2,0:T(8,128)(2,1)S(1)} async-done(((bf16[16,256,256]{1,2,0:T(8,128)(2,1)}), bf16[16,256,256]{1,2,0:T(8,128)(2,1)S(1)}, u32[]{:S(2)}, u32[]{:S(2)}) %all-to-all-start.2) | async-done | bytes 2097184 | tf_op jit(solution)/shard_map/all_to_all | solution.py:138
  324.6 2.8 copy.99
  327.4 0.8 slice.19
  328.3 0.6 convert_element_type.49
  328.9 0.7 broadcast_select_fusion.4
  (79 shorter events, 1.1 us)
Async XLA Ops:
  2.0 12.4 %all-to-all-start.1 = ((bf16[256,16,4]{0,2,1:T(4,128)(2,1)}), bf16[256,16,4]{0,2,1:T(4,128)(2,1)S(1)}, u32[]{:S(2)}, u32[]{:S(2)}) async-start(bf16[256,16,4]{0,2,1:T(4,128)(2,1)} %reshape.136), calls=%async_computation.1 | async-start | bytes 65536 | tf_op jit(solution)/shard_map/all_to_all | solution.py:131
  14.4 6.0 %copy-start.15 = (bf16[256,128]{1,0:T(8,128)(2,1)S(1)}, bf16[256,128]{1,0:T(8,128)(2,1)}, u32[]{:S(2)}) copy-start(bf16[256,128]{1,0:T(8,128)(2,1)} %param.8) | copy-start | bytes 196612
  14.4 6.0 %copy-start.16 = (bf16[256,128]{1,0:T(8,128)(2,1)S(1)}, bf16[256,128]{1,0:T(8,128)(2,1)}, u32[]{:S(2)}) copy-start(bf16[256,128]{1,0:T(8,128)(2,1)} %param.9) | copy-start | bytes 196612
  14.4 75.7 %all-to-all-start.3 = ((bf16[256,16,256]{0,2,1:T(8,128)(2,1)}), bf16[256,16,256]{0,2,1:T(8,128)(2,1)S(1)}, u32[]{:S(2)}, u32[]{:S(2)}) async-start(bf16[256,16,256]{0,2,1:T(8,128)(2,1)} %bitcast.189), calls=%async_computation.3 | async-start | bytes 4194304 | tf_op jit(solution)/shard_map/all_to_all | solution.py:125
  20.4 8.2 %collective-permute-start = (bf16[256,128]{1,0:T(8,128)(2,1)S(1)}, bf16[256,128]{1,0:T(8,128)(2,1)S(1)}, u32[]{:S(2)}, u32[]{:S(2)}) collective-permute-start(bf16[256,128]{1,0:T(8,128)(2,1)S(1)} %broadcast_select_fusion.6), channel_id=1, source_target_pairs={{0,2},{2,0},{4,6},{6,4},{8,10},{10,8},{12,14},{14,12},{16,18},{18,... | collective-permute-start | bytes 196616 | tf_op jit(solution)/shard_map/ppermute | solution.py:87
  28.7 5.8 %collective-permute-start.1 = (bf16[512,128]{1,0:T(8,128)(2,1)S(1)}, bf16[512,128]{1,0:T(8,128)(2,1)S(1)}, u32[]{:S(2)}, u32[]{:S(2)}) collective-permute-start(bf16[512,128]{1,0:T(8,128)(2,1)S(1)} %maximum_select_fusion.3), channel_id=1, source_target_pairs={{0,4},{2,6},{4,0},{6,2},{8,12},{10,14},{12,8},{14,10},{16,20},{18,... | collective-permute-start | bytes 393224 | tf_op jit(solution)/shard_map/ppermute | solution.py:87
  34.5 25.5 %collective-permute-start.2 = (bf16[1024,128]{1,0:T(8,128)(2,1)S(1)}, bf16[1024,128]{1,0:T(8,128)(2,1)S(1)}, u32[]{:S(2)}, u32[]{:S(2)}) collective-permute-start(bf16[1024,128]{1,0:T(8,128)(2,1)S(1)} %maximum_select_fusion.2), channel_id=1, source_target_pairs={{0,8},{2,10},{4,12},{6,14},{8,0},{10,2},{12,4},{14,6},{16,24},{18,... | collective-permute-start | bytes 786440 | tf_op jit(solution)/shard_map/ppermute | solution.py:87
  60.2 7.7 %copy-start.14 = (bf16[2048,128]{1,0:T(8,128)(2,1)}, bf16[2048,128]{1,0:T(8,128)(2,1)S(1)}, u32[]{:S(2)}) copy-start(bf16[2048,128]{1,0:T(8,128)(2,1)S(1)} %maximum_select_fusion.1) | copy-start | bytes 1572868
  60.2 28.0 %collective-permute-start.3 = (bf16[2048,128]{1,0:T(8,128)(2,1)S(1)}, bf16[2048,128]{1,0:T(8,128)(2,1)}, u32[]{:S(2)}, u32[]{:S(2)}) collective-permute-start(bf16[2048,128]{1,0:T(8,128)(2,1)S(1)} %maximum_select_fusion.1), channel_id=1, source_target_pairs={{0,16},{2,18},{4,20},{6,22},{8,24},{10,26},{12,28},{14,30},{16,0},... | collective-permute-start | bytes 1572872 | tf_op jit(solution)/shard_map/ppermute | solution.py:87
  90.1 8.2 %copy-start.27 = (f32[64]{0:T(128)S(1)}, f32[64]{0:T(128)}, u32[]{:S(2)}) copy-start(f32[64]{0:T(128)} %param.11) | copy-start | bytes 772
  90.1 8.1 %copy-start.7 = (bf16[256,16,256]{0,2,1:T(8,128)(2,1)}, bf16[256,16,256]{0,2,1:T(8,128)(2,1)S(1)}, u32[]{:S(2)}) copy-start(bf16[256,16,256]{0,2,1:T(8,128)(2,1)S(1)} %all-to-all-done.3) | copy-start | bytes 6291460
  90.1 54.6 %all-to-all-start = ((bf16[256,16,256]{0,2,1:T(8,128)(2,1)}), bf16[256,16,256]{0,2,1:T(8,128)(2,1)}, u32[]{:S(2)}, u32[]{:S(2)}) async-start(bf16[256,16,256]{0,2,1:T(8,128)(2,1)} %bitcast.190), calls=%async_computation | async-start | bytes 4194304 | tf_op jit(solution)/shard_map/all_to_all | solution.py:128
  98.3 0.9 copy-start.25
  98.4 2.7 collective-permute-start.4
  99.4 53.6 %copy-start.17 = (f32[4,16,256]{2,1,0:T(8,128)}, f32[4,16,256]{2,1,0:T(8,128)S(1)}, u32[]{:S(2)}) copy-start(f32[4,16,256]{2,1,0:T(8,128)S(1)} %get-tuple-element.36) | copy-start | bytes 196612
  101.2 4.5 %copy-start.5 = (bf16[4096,128]{1,0:T(8,128)(2,1)}, bf16[4096,128]{1,0:T(8,128)(2,1)S(1)}, u32[]{:S(2)}) copy-start(bf16[4096,128]{1,0:T(8,128)(2,1)S(1)} %get-tuple-element.27) | copy-start | bytes 3145732
  102.9 2.8 copy-start.8
  158.9 2.0 copy-start.9
  160.9 4.0 %copy-start.2 = (bf16[4096,4,64]{0,2,1:T(8,128)(2,1)S(1)}, bf16[4096,4,64]{0,2,1:T(8,128)(2,1)}, u32[]{:S(2)}) copy-start(bf16[4096,4,64]{0,2,1:T(8,128)(2,1)} %reshape.135) | copy-start | bytes 6291460
  160.9 4.0 %copy-start.12 = (f32[16,256,256]{2,1,0:T(8,128)S(1)}, f32[16,256,256]{2,1,0:T(8,128)}, u32[]{:S(2)}) copy-start(f32[16,256,256]{2,1,0:T(8,128)} %fusion.112) | copy-start | bytes 12582916
  160.9 4.0 %copy-start.22 = (f32[1,4,16,256]{3,2,1,0:T(8,128)S(1)}, f32[1,4,16,256]{3,2,1,0:T(8,128)}, u32[]{:S(2)}) copy-start(f32[1,4,16,256]{3,2,1,0:T(8,128)} %copy.227) | copy-start | bytes 196612
  187.5 2.7 copy-start.23
  188.8 1.3 copy-start
  190.1 2.0 copy-start.13
  190.2 2.0 copy-start.18
  199.4 3.7 %copy-start.4 = (f32[16,256,256]{2,1,0:T(8,128)S(1)}, f32[16,256,256]{2,1,0:T(8,128)}, u32[]{:S(2)}) copy-start(f32[16,256,256]{2,1,0:T(8,128)} %get-tuple-element.17) | copy-start | bytes 12582916
  199.4 3.7 %copy-start.6 = (bf16[4096,128]{1,0:T(8,128)(2,1)S(1)}, bf16[4096,128]{1,0:T(8,128)(2,1)}, u32[]{:S(2)}) copy-start(bf16[4096,128]{1,0:T(8,128)(2,1)} %copy-done.5) | copy-start | bytes 3145732
  199.4 4.4 %copy-start.11 = (f32[16,256,128,1]{2,1,3,0:T(8,128)S(1)}, f32[16,256,128,1]{2,1,3,0:T(8,128)}, u32[]{:S(2)}) copy-start(f32[16,256,128,1]{2,1,3,0:T(8,128)} %fusion.9) | copy-start | bytes 6291460
  203.8 3.9 %copy-start.1 = (f32[16,4,64,128]{3,2,1,0:T(8,128)S(1)}, f32[16,4,64,128]{3,2,1,0:T(8,128)}, u32[]{:S(2)}) copy-start(f32[16,4,64,128]{3,2,1,0:T(8,128)} %copy-done) | copy-start | bytes 6291460
  203.8 3.9 %copy-start.10 = (f32[4,16,64,128]{3,2,1,0:T(8,128)S(1)}, f32[4,16,64,128]{3,2,1,0:T(8,128)}, u32[]{:S(2)}) copy-start(f32[4,16,64,128]{3,2,1,0:T(8,128)} %copy-done.9) | copy-start | bytes 6291460
  207.6 3.8 %copy-start.24 = (f32[4,16]{1,0:T(4,128)S(1)}, f32[4,16]{1,0:T(4,128)}, u32[]{:S(2)}) copy-start(f32[4,16]{1,0:T(4,128)} %get-tuple-element.31) | copy-start | bytes 772
  207.6 3.8 %copy-start.29 = (f32[4,16]{1,0:T(4,128)S(1)}, f32[4,16]{1,0:T(4,128)}, u32[]{:S(2)}) copy-start(f32[4,16]{1,0:T(4,128)} %get-tuple-element.41) | copy-start | bytes 772
  207.6 4.1 %copy-start.19 = (f32[4,16,256]{2,1,0:T(8,128)S(1)}, f32[4,16,256]{2,1,0:T(8,128)}, u32[]{:S(2)}) copy-start(f32[4,16,256]{2,1,0:T(8,128)} %get-tuple-element.14) | copy-start | bytes 196612
  207.6 4.1 %copy-start.20 = (f32[4,16,256]{2,1,0:T(8,128)S(1)}, f32[4,16,256]{2,1,0:T(8,128)}, u32[]{:S(2)}) copy-start(f32[4,16,256]{2,1,0:T(8,128)} %get-tuple-element.15) | copy-start | bytes 196612
  207.6 4.1 %copy-start.21 = (f32[4,16,256]{2,1,0:T(8,128)S(1)}, f32[4,16,256]{2,1,0:T(8,128)}, u32[]{:S(2)}) copy-start(f32[4,16,256]{2,1,0:T(8,128)} %get-tuple-element.19) | copy-start | bytes 196612
  207.6 4.4 %copy-start.26 = (f32[4]{0:T(128)S(1)}, f32[4]{0:T(128)}, u32[]{:S(2)}) copy-start(f32[4]{0:T(128)} %copy-done.25) | copy-start | bytes 52
  207.6 4.6 %collective-permute-start.5 = (f32[4096,128]{1,0:T(8,128)}, f32[4096,128]{1,0:T(8,128)}, u32[]{:S(2)}, u32[]{:S(2)}) collective-permute-start(f32[4096,128]{1,0:T(8,128)} %bitcast.34), channel_id=1, source_target_pairs={{0,1},{1,0},{2,3},{3,2},{4,5},{5,4},{6,7},{7,6},{8,9},{9,8},{10,11... | collective-permute-start | bytes 6291464 | tf_op jit(solution)/shard_map/ppermute | solution.py:150
  215.6 5.7 %copy-start.28 = (f32[64]{0:T(128)S(1)}, f32[64]{0:T(128)}, u32[]{:S(2)}) copy-start(f32[64]{0:T(128)} %param.12) | copy-start | bytes 772
  215.6 5.8 %copy-start.3 = (bf16[4096,4,64]{0,2,1:T(8,128)(2,1)S(1)}, bf16[4096,4,64]{0,2,1:T(8,128)(2,1)}, u32[]{:S(2)}) copy-start(bf16[4096,4,64]{0,2,1:T(8,128)(2,1)} %reshape.135) | copy-start | bytes 6291460
  215.6 55.4 %all-to-all-start.4 = ((f32[16,264,128]{2,1,0:T(8,128)}), f32[16,264,128]{2,1,0:T(8,128)}, u32[]{:S(2)}, u32[]{:S(2)}) async-start(f32[16,264,128]{2,1,0:T(8,128)} %pad_maximum_fusion), calls=%async_computation.4 | async-start | bytes 4325376 | tf_op jit(solution)/shard_map/all_to_all | solution.py:157
  271.0 53.6 %all-to-all-start.2 = ((bf16[16,256,256]{1,2,0:T(8,128)(2,1)}), bf16[16,256,256]{1,2,0:T(8,128)(2,1)S(1)}, u32[]{:S(2)}, u32[]{:S(2)}) async-start(bf16[16,256,256]{1,2,0:T(8,128)(2,1)} %copy.82), calls=%async_computation.2 | async-start | bytes 4194304 | tf_op jit(solution)/shard_map/all_to_all | solution.py:138
  278.4 50.5 %collective-permute-start.6 = (f32[256,128]{1,0:T(8,128)S(1)}, f32[256,128]{1,0:T(8,128)S(1)}, u32[]{:S(2)}, u32[]{:S(2)}) collective-permute-start(f32[256,128]{1,0:T(8,128)S(1)} %slice_reduce_fusion), channel_id=1, source_target_pairs={{0,1},{1,0},{2,3},{3,2},{4,5},{5,4},{6,7},{7,6},{8,9},{9,8},{10,11... | collective-permute-start | bytes 393224 | tf_op jit(solution)/shard_map/ppermute | solution.py:167
where the time goes:
time: 333 us; the launch traced here: 330 us
  waiting for transfers between devices  173 us (52%)
  matrix products  66.2 us (20%)
  starting transfers between devices  41.4 us (12%)
  local copies, waits for them, and re-layouts  37.9 us (11%)
  other arithmetic  9.84 us (3%)
    ppermute x4, waiting for transfers between devices, gather_ctx(): theirs = lax.ppermute(have, 'ctx', [(k, k ^ step) for k in range(owners)])  54.9 us
    all_to_all x1, waiting for transfers between devices, local(): lax.all_to_all(x_back, 'ctx', split_axis=0, concat_axis=1, tiled=True)  46.1 us
    all_to_all x1, waiting for transfers between devices, local(): lax.all_to_all(packed, 'ctx', split_axis=0, concat_axis=0, tiled=True)  36.7 us
    all_to_all x1, waiting for transfers between devices, local(): lax.all_to_all(g_in, 'ctx', split_axis=1, concat_axis=0, tiled=True)  33.6 us
    dot_general x2, matrix products, head_forward(): output = jnp.einsum('kij,kjp->kip', scores, x_blocks, precision=precise)  25.5 us
    unnamed x67, local copies, waits for them, and re-layouts  14.5 us
    dot_general x2, matrix products, head_forward(): jnp.einsum('kin,kpn->kip', reading, entering, precision=precise)  11 us
    dot_general x3, matrix products, head_forward(): states = jnp.einsum('kjp,kjn->kpn', weighted, b_blocks, precision=precise)  10.5 us
  transfers between devices with their start and end apart: 12, of which 9 were waited for; matrix products, arithmetic and copies ran while one was open for 14% of the time, Pallas kernels for 0%

commit v1 on v0

--- a/solution.py
+++ b/solution.py
@@ -6,6 +6,29 @@
 
 BLOCK = 256
 precise = lax.Precision.HIGH
+
+
+def cut_along(value, dim, length):
+    dims = value.shape
+    pieces = value.reshape(*dims[:dim], length, dims[dim] // length, *dims[dim + 1 :])
+    return jnp.moveaxis(pieces, dim, 0)
+
+
+def joined_along(pieces, dim):
+    shape = list(pieces.shape[1:])
+    shape[dim] *= pieces.shape[0]
+    return jnp.moveaxis(pieces, 0, dim).reshape(shape)
+
+
+def swapped_with_each(x, axis, split_dim, concat_dim):
+    size, place = (lax.axis_size(axis), lax.axis_index(axis))
+    blocks = cut_along(x, split_dim, size)
+    done = [blocks[place]]
+    for lap in range(1, size):
+        sent = blocks[place ^ lap]
+        done.append(lax.ppermute(sent, axis, [(i, i ^ lap) for i in range(size)]))
+    blocks = jnp.stack(done)[place ^ jnp.arange(size)]
+    return joined_along(blocks, concat_dim)
 
 
 def head_forward(x_head, b_rows, c_rows, raw_step, log_rate, skip_gain, start_state, block_len):
@@ -134,11 +157,7 @@
         x_back, raw_back, gb, gc = chunk_backward(
             x_seq, g_seq, raw_seq, b_rows, c_rows, rate_own[sl], gain_own[sl]
         )
-        x_parts.append(
-            lax.all_to_all(x_back, "ctx", split_axis=0, concat_axis=1, tiled=True).reshape(
-                rows, owners, 1, width
-            )
-        )
+        x_parts.append(swapped_with_each(x_back, "ctx", 0, 1).reshape(rows, owners, 1, width))
         raw_parts.append(raw_back)
         grad_b_all = gb if grad_b_all is None else grad_b_all + gb
         grad_c_all = gc if grad_c_all is None else grad_c_all + gc

time: 333 us -> 348 us (1.045)
  the two profiles are of different devices: /device:TPU:12 before, /device:TPU:9 now
where the time goes in v1:
time: 348 us; the launch traced here: 345 us
  waiting for transfers between devices  131 us (38%)
  local copies, waits for them, and re-layouts  73.2 us (21%)
  matrix products  65.6 us (19%)
  starting transfers between devices  60.3 us (17%)
  other arithmetic  13.1 us (4%)
    ppermute x4, waiting for transfers between devices, gather_ctx(): theirs = lax.ppermute(have, 'ctx', [(k, k ^ step) for k in range(owners)])  57 us
    ppermute x15, waiting for transfers between devices, swapped_with_each(): done.append(lax.ppermute(sent, axis, [(i, i ^ lap) for i in range(size)]))  43 us
    unnamed x89, local copies, waits for them, and re-layouts  31 us
    all_to_all x1, waiting for transfers between devices, local(): lax.all_to_all(g_in, 'ctx', split_axis=1, concat_axis=0, tiled=True)  29.6 us
    dot_general x2, matrix products, head_forward(): output = jnp.einsum('kij,kjp->kip', scores, x_blocks, precision=precise)  24.1 us
    ppermute x15, starting transfers between devices, swapped_with_each(): done.append(lax.ppermute(sent, axis, [(i, i ^ lap) for i in range(size)]))  20.6 us
    dynamic_slice x16, local copies, waits for them, and re-layouts, swapped_with_each(): sent = blocks[place ^ lap]  12.9 us
    dot_general x3, matrix products, head_forward(): jnp.einsum('kin,kjn->kij', c_blocks, b_blocks, precision=precise)  11 us
  transfers between devices with their start and end apart: 26, of which 17 were waited for; matrix products, arithmetic and copies ran while one was open for 24% of the time, Pallas kernels for 0%

profile of v1, /device:TPU:9, one launch (start us, length us, event | category | flops | bytes accessed | tf_op | source)
XLA Modules:
  0.0 344.8 jit_solution(3173415457969885157)
XLA Ops:
  0.6 1.4 reshape.150
  2.0 6.7 %all-to-all-start.1 = ((bf16[256,16,4]{0,2,1:T(4,128)(2,1)}), bf16[256,16,4]{0,2,1:T(4,128)(2,1)S(1)}, u32[]{:S(2)}, u32[]{:S(2)}) async-start(bf16[256,16,4]{0,2,1:T(4,128)(2,1)} %reshape.150), calls=%async_computation.1 | async-start | bytes 65536 | tf_op jit(solution)/shard_map/all_to_all | solution.py:154
  8.7 4.1 %copy.131 = bf16[256,4096]{0,1:T(8,128)(2,1)} copy(bf16[256,4096]{1,0:T(8,128)(2,1)} %param.7) | data formatting | bytes 4194304 | tf_op args[0]
  13.9 5.4 %all-to-all-start.2 = ((bf16[256,16,256]{0,2,1:T(8,128)(2,1)}), bf16[256,16,256]{0,2,1:T(8,128)(2,1)S(1)}, u32[]{:S(2)}, u32[]{:S(2)}) async-start(bf16[256,16,256]{0,2,1:T(8,128)(2,1)} %bitcast.236), calls=%async_computation.2 | async-start | bytes 4194304 | tf_op jit(solution)/shard_map/all_to_all | solution.py:148
  20.5 6.9 %collective-permute-done = bf16[256,128]{1,0:T(8,128)(2,1)S(1)} collective-permute-done((bf16[256,128]{1,0:T(8,128)(2,1)S(1)}, bf16[256,128]{1,0:T(8,128)(2,1)S(1)}, u32[]{:S(2)}, u32[]{:S(2)}) %collective-permute-start) | collective-permute-done | bytes 65568 | tf_op jit(solution)/shard_map/ppermute | solution.py:110
  28.3 4.2 %collective-permute-done.1 = bf16[512,128]{1,0:T(8,128)(2,1)S(1)} collective-permute-done((bf16[512,128]{1,0:T(8,128)(2,1)S(1)}, bf16[512,128]{1,0:T(8,128)(2,1)S(1)}, u32[]{:S(2)}, u32[]{:S(2)}) %collective-permute-start.1) | collective-permute-done | bytes 131104 | tf_op jit(solution)/shard_map/ppermute | solution.py:110
  32.6 1.8 collective-permute-start.2
  34.4 24.0 %collective-permute-done.2 = bf16[1024,128]{1,0:T(8,128)(2,1)S(1)} collective-permute-done((bf16[1024,128]{1,0:T(8,128)(2,1)S(1)}, bf16[1024,128]{1,0:T(8,128)(2,1)S(1)}, u32[]{:S(2)}, u32[]{:S(2)}) %collective-permute-start.2) | collective-permute-done | bytes 262176 | tf_op jit(solution)/shard_map/ppermute | solution.py:110
  59.8 4.1 %copy.102 = bf16[256,4096]{0,1:T(8,128)(2,1)} copy(bf16[256,4096]{1,0:T(8,128)(2,1)} %param.13) | data formatting | bytes 4194304 | tf_op args[6]
  63.9 21.8 %collective-permute-done.3 = bf16[2048,128]{1,0:T(8,128)(2,1)} collective-permute-done((bf16[2048,128]{1,0:T(8,128)(2,1)S(1)}, bf16[2048,128]{1,0:T(8,128)(2,1)}, u32[]{:S(2)}, u32[]{:S(2)}) %collective-permute-start.3) | collective-permute-done | bytes 524320 | tf_op jit(solution)/shard_map/ppermute | solution.py:110
  85.7 1.8 maximum_select_fusion
  87.6 9.1 %all-to-all-start = ((bf16[256,16,256]{0,2,1:T(8,128)(2,1)}), bf16[256,16,256]{0,2,1:T(8,128)(2,1)}, u32[]{:S(2)}, u32[]{:S(2)}) async-start(bf16[256,16,256]{0,2,1:T(8,128)(2,1)} %bitcast.237), calls=%async_computation | async-start | bytes 4194304 | tf_op jit(solution)/shard_map/all_to_all | solution.py:151
  98.1 2.5 collective-permute-start.4
  103.0 1.7 copy.105
  104.7 2.7 fusion.113
  107.4 2.5 copy.132
  109.9 2.9 reshape.156
  112.8 29.6 %all-to-all-done = bf16[256,16,256]{0,2,1:T(8,128)(2,1)} async-done(((bf16[256,16,256]{0,2,1:T(8,128)(2,1)}), bf16[256,16,256]{0,2,1:T(8,128)(2,1)}, u32[]{:S(2)}, u32[]{:S(2)}) %all-to-all-start) | async-done | bytes 2097184 | tf_op jit(solution)/shard_map/all_to_all | solution.py:151
  142.4 4.1 %copy.103 = bf16[16,256,1,256]{1,0,3,2:T(8,128)(2,1)} copy(bf16[16,256,1,256]{1,3,0,2:T(8,128)(2,1)} %bitcast.2) | data formatting | bytes 4194304 | tf_op jit(solution)/shard_map/all_to_all | solution.py:151
  146.4 4.2 %reshape.149 = bf16[4096,4,64]{0,2,1:T(8,128)(2,1)} reshape(bf16[16,256,1,256]{1,0,3,2:T(8,128)(2,1)} %copy.103) | data formatting | bytes 4194304 | tf_op jit(solution)/shard_map/reshape | solution.py:151
  150.7 5.9 %multiply_reduce_fusion.4 = (f32[4,16]{1,0:T(4,128)}, f32[4,16,64,128]{3,2,1,0:T(8,128)S(1)}) fusion(f32[16,256,128]{1,2,0:T(8,128)} %copy.105, f32[4,16,256]{2,1,0:T(8,128)S(1)} %get-tuple-element.52, bf16[4,8,16,8,256]{4,3,2,1,0:T(8,128)(2,1)} %bitcast.226), kind=kOutput, calls=%fused_computation.43 | convolution fusion | flops 808452032 | bytes 6357248 | tf_op jit(solution)/shard_map/transpose(jvp(vmap(kin,kpn->kip)))/dot_general | solution.py:71
  156.5 2.0 fusion.44
  158.6 3.9 %fusion.10 = (f32[4,16,256]{2,0,1:T(4,128)S(1)}, f32[16,4,64,256]{3,2,1,0:T(8,128)}) fusion(bf16[4,8,16,8,256]{4,3,2,1,0:T(8,128)(2,1)S(1)} %bitcast.217, bf16[16,256,128,1]{2,1,3,0:T(8,128)(2,1)S(1)} %bitcast.222, f32[16,4,64,128]{3,0,2,1:T(8,128)S(1)} %fusion.44), kind=kOutput, calls=%fused_computation.19 | convolution fusion | flops 808435712 | bytes 9502720 | tf_op jit(solution)/shard_map/transpose(jvp(vmap(kjp,kjn->kpn)))/dot_general | solution.py:58
  162.5 16.3 %fusion.5 = (f32[4,16,256]{2,1,0:T(8,128)}, f32[4,16,256]{2,1,0:T(8,128)}, f32[4,16,256]{2,1,0:T(8,128)S(1)}, f32[16,256,256]{2,1,0:T(8,128)}, f32[4,16,256,256]{3,2,1,0:T(8,128)}) fusion(f32[4,16,256]{2,1,0:T(8,128)S(1)} %bitcast.264, f32[4,16,256]{2,1,0:T(8,128)S(1)} %get-tuple-element.53, f32[16,256,256]{2,1,0:T(8,128)S(1)} %copy-done.13, ...), kind=kOutput, calls=%fused_computation.10 | convolution fusion | flops 594493440 | bytes 29753344 | tf_op jit(solution)/shard_map/transpose(jvp(vmap(kij,kjp->kip)))/dot_general | solution.py:55
  181.0 5.2 %fusion.9 = f32[16,256,128,1]{2,1,3,0:T(8,128)} fusion(f32[4,16,256]{2,0,1:T(4,128)S(1)} %copy.104, f32[16,4,64,128]{3,0,2,1:T(8,128)S(1)} %fusion.44, bf16[4,8,16,8,256]{4,3,2,1,0:T(8,128)(2,1)S(1)} %bitcast.220), kind=kOutput, calls=%fused_computation.18 | convolution fusion | flops 807403520 | bytes 6356992 | tf_op jit(solution)/shard_map/transpose(jvp(vmap(kjp,kjn->kpn)))/dot_general | solution.py:58
  186.3 2.0 fusion.47
  188.3 5.1 %multiply_reduce_fusion.3 = (f32[16,256,128]{1,2,0:T(8,128)}, f32[4,16,256]{2,1,0:T(8,128)}) fusion(f32[4,16,256]{2,1,0:T(8,128)S(1)} %copy-done.21, f32[16,256,128]{1,2,0:T(8,128)S(1)} %copy-done.14, f32[4,16,64,128]{3,1,2,0:T(8,128)S(1)} %fusion.47, bf16[4,8,16,8,256]{4,3,2,1,0:T(8,128)(2,1)S(1)} %bitcast.228), kind=kOutput, calls=%fused_computation.12 | convolution fusion | flops 813154304 | bytes 8519680 | tf_op jit(solution)/shard_map/transpose(jvp(vmap(kin,kpn->kip)))/dot_general | solution.py:71
  193.4 2.1 copy.141
  195.6 3.7 %convolution_add_fusion = f32[16,256,128]{2,1,0:T(8,128)S(1)} fusion(f32[16,256,128]{2,1,0:T(8,128)S(1)} %copy.141, f32[16,256,256]{2,1,0:T(8,128)} %get-tuple-element.17, bf16[16,256,128]{2,1,0:T(8,128)(2,1)S(1)} %bitcast.224), kind=kOutput, calls=%fused_computation.58 | convolution fusion | flops 805830656 | bytes 9437184 | tf_op jit(solution)/shard_map/transpose(jvp(vmap(kin,kjn->kij)))/dot_general | solution.py:51
  200.0 4.7 %broadcast_select_fusion.1 = (f32[16,256,128]{2,1,0:T(8,128)}, f32[16,256,128]{2,1,0:T(8,128)}) fusion(f32[16,256,128]{2,1,0:T(8,128)S(1)} %convolution_add_fusion, pred[]{:T(512)S(6)} %eq.35, f32[16,256,256]{2,1,0:T(8,128)S(1)} %copy-done.5, bf16[16,256,128]{2,1,0:T(8,128)(2,1)S(1)} %bitcast.233, f32[16,256,128,1]{2,1,3,0:T(8,128)S(1)} %copy-done.12), kind=kOutput, calls=%fused_computation.73 | convolution fusion | flops 806879232 | bytes 13631489 | tf_op jit(solution)/shard_map/transpose(jvp(vmap(kin,kjn->kij)))/dot_general | solution.py:51
  204.6 2.4 collective-permute-start.20
  207.0 7.8 %fusion.12 = f32[16,4,8,8,256]{4,3,2,1,0:T(8,128)S(1)} fusion(f32[16,4,64,256]{3,2,1,0:T(8,128)S(1)} %copy-done.4, f32[4,16,256]{2,0,1:T(4,128)S(1)} %copy.104, bf16[4,8,16,8,256]{4,3,2,1,0:T(8,128)(2,1)S(1)} %bitcast.229, f32[4,16,256,256]{3,2,1,0:T(8,128)} %get-tuple-element.24), kind=kOutput, calls=%fused_computation.22 | convolution fusion | flops 1612709888 | bytes 27328512 | tf_op jit(solution)/shard_map/transpose(jvp(vmap(kij,kjp->kip)))/dot_general | solution.py:55
  214.8 2.6 copy.166
  218.6 3.7 %fusion.111 = (f32[4,16]{1,0:T(4,128)S(1)}, f32[4,16]{1,0:T(4,128)S(1)}) fusion(f32[4,16]{1,0:T(4,128)S(1)} %get-tuple-element.54, f32[4,16]{1,0:T(4,128)S(1)} %get-tuple-element.23, f32[16,4,64,128]{3,2,1,0:T(8,128)S(1)} %copy-done.1, f32[4,16,64,128]{3,2,1,0:T(8,128)S(1)} %copy-done.11, pred[16,16]{1,0:T(8,128)(4,1)S(1)} %iota_compare_fusion.6), kind=kOutput, calls=%fused_computation.172 | convolution fusion | flops 50337664 | bytes 4195584 | tf_op jit(solution)/shard_map/transpose(jvp(vmap(kj,jpn->kpn)))/dot_general | solution.py:67
  223.0 2.4 bitcast_add_fusion.1
  225.5 1.6 pad_maximum_fusion
  227.0 6.1 %all-to-all-start.3 = ((f32[16,264,128]{2,1,0:T(8,128)}), f32[16,264,128]{2,1,0:T(8,128)}, u32[]{:S(2)}, u32[]{:S(2)}) async-start(f32[16,264,128]{2,1,0:T(8,128)} %pad_maximum_fusion), calls=%async_computation.3 | async-start | bytes 4325376 | tf_op jit(solution)/shard_map/all_to_all | solution.py:176
  233.1 2.9 fusion.13
  236.6 6.3 %constant_dynamic-slice_fusion = (bf16[1,256,256]{1,0,2:T(2,128)(2,1)S(1)}, bf16[1,256,256]{1,0,2:T(2,128)(2,1)S(1)}, bf16[1,256,256]{1,0,2:T(2,128)(2,1)S(1)}, ...) fusion(bf16[16,256,256]{1,0,2:T(8,128)(2,1)S(1)} %bitcast.225, ...), kind=kLoop, calls=%fused_computation.142 | loop fusion | bytes 4194368 | tf_op jit(solution)/shard_map/dynamic_slice | solution.py:28
  242.9 1.7 copy.115
  246.9 1.7 copy.116
  251.8 2.4 collective-permute-start.9
  257.6 1.6 bitcast_dynamic-update-slice_fusion.14
  260.3 1.6 bitcast_dynamic-update-slice_fusion.13
  261.9 5.0 %collective-permute-done.7 = bf16[256,256]{1,0:T(8,128)(2,1)} collective-permute-done((bf16[256,256]{1,0:T(8,128)(2,1)}, bf16[256,256]{1,0:T(8,128)(2,1)}, u32[]{:S(2)}, u32[]{:S(2)}) %collective-permute-start.7) | collective-permute-done | bytes 131104 | tf_op jit(solution)/shard_map/ppermute | solution.py:29
  266.9 1.6 bitcast_dynamic-update-slice_fusion.12
  268.5 4.5 %collective-permute-done.8 = bf16[256,256]{1,0:T(8,128)(2,1)} collective-permute-done((bf16[256,256]{1,0:T(8,128)(2,1)}, bf16[256,256]{1,0:T(8,128)(2,1)}, u32[]{:S(2)}, u32[]{:S(2)}) %collective-permute-start.8) | collective-permute-done | bytes 131104 | tf_op jit(solution)/shard_map/ppermute | solution.py:29
  273.7 1.6 bitcast_dynamic-update-slice_fusion.11
  276.0 2.9 collective-permute-start.14
  278.8 1.6 bitcast_dynamic-update-slice_fusion.10
  282.2 3.2 collective-permute-done.11
  287.1 11.2 %collective-permute-done.12 = bf16[256,256]{1,0:T(8,128)(2,1)S(1)} collective-permute-done((bf16[256,256]{1,0:T(8,128)(2,1)S(1)}, bf16[256,256]{1,0:T(8,128)(2,1)S(1)}, u32[]{:S(2)}, u32[]{:S(2)}) %collective-permute-start.12) | collective-permute-done | bytes 131104 | tf_op jit(solution)/shard_map/ppermute | solution.py:29
  298.3 2.0 collective-permute-start.17
  301.1 3.8 %collective-permute-start.18 = (bf16[256,256]{1,0:T(8,128)(2,1)S(1)}, bf16[256,256]{1,0:T(8,128)(2,1)S(1)}, u32[]{:S(2)}, u32[]{:S(2)}) collective-permute-start(bf16[256,256]{1,0:T(8,128)(2,1)S(1)} %bitcast.251), channel_id=1, source_target_pairs={{0,28},{2,30},{4,24},{6,26},{8,20},{10,22},{12,16},{14,18},{16,12}... | collective-permute-start | bytes 393224 | tf_op jit(solution)/shard_map/ppermute | solution.py:29
  305.5 1.7 collective-permute-start.19
  307.9 3.2 collective-permute-done.15
  311.7 7.6 %collective-permute-done.16 = bf16[256,256]{1,0:T(8,128)(2,1)S(1)} collective-permute-done((bf16[256,256]{1,0:T(8,128)(2,1)S(1)}, bf16[256,256]{1,0:T(8,128)(2,1)S(1)}, u32[]{:S(2)}, u32[]{:S(2)}) %collective-permute-start.16) | collective-permute-done | bytes 131104 | tf_op jit(solution)/shard_map/ppermute | solution.py:29
  319.9 3.5 %collective-permute-done.17 = bf16[256,256]{1,0:T(8,128)(2,1)S(1)} collective-permute-done((bf16[256,256]{1,0:T(8,128)(2,1)S(1)}, bf16[256,256]{1,0:T(8,128)(2,1)S(1)}, u32[]{:S(2)}, u32[]{:S(2)}) %collective-permute-start.17) | collective-permute-done | bytes 131104 | tf_op jit(solution)/shard_map/ppermute | solution.py:29
  324.1 3.9 %collective-permute-done.18 = bf16[256,256]{1,0:T(8,128)(2,1)S(1)} collective-permute-done((bf16[256,256]{1,0:T(8,128)(2,1)S(1)}, bf16[256,256]{1,0:T(8,128)(2,1)S(1)}, u32[]{:S(2)}, u32[]{:S(2)}) %collective-permute-start.18) | collective-permute-done | bytes 131104 | tf_op jit(solution)/shard_map/ppermute | solution.py:29
  328.7 1.7 slice_reduce_fusion
  330.4 2.5 collective-permute-start.21
  333.6 2.3 gather_fusion
  335.8 2.4 copy.130
  338.2 4.1 %copy.147 = bf16[256,4096]{1,0:T(8,128)(2,1)} copy(bf16[256,4096]{0,1:T(8,128)(2,1)} %bitcast.239) | data formatting | bytes 4194304
  (149 shorter events, 36.3 us)
Async XLA Ops:
  2.0 11.9 %all-to-all-start.1 = ((bf16[256,16,4]{0,2,1:T(4,128)(2,1)}), bf16[256,16,4]{0,2,1:T(4,128)(2,1)S(1)}, u32[]{:S(2)}, u32[]{:S(2)}) async-start(bf16[256,16,4]{0,2,1:T(4,128)(2,1)} %reshape.150), calls=%async_computation.1 | async-start | bytes 65536 | tf_op jit(solution)/shard_map/all_to_all | solution.py:154
  13.9 5.4 %copy-start.16 = (bf16[256,128]{1,0:T(8,128)(2,1)S(1)}, bf16[256,128]{1,0:T(8,128)(2,1)}, u32[]{:S(2)}) copy-start(bf16[256,128]{1,0:T(8,128)(2,1)} %param.8) | copy-start | bytes 196612
  13.9 5.4 %copy-start.17 = (bf16[256,128]{1,0:T(8,128)(2,1)S(1)}, bf16[256,128]{1,0:T(8,128)(2,1)}, u32[]{:S(2)}) copy-start(bf16[256,128]{1,0:T(8,128)(2,1)} %param.9) | copy-start | bytes 196612
  13.9 73.7 %all-to-all-start.2 = ((bf16[256,16,256]{0,2,1:T(8,128)(2,1)}), bf16[256,16,256]{0,2,1:T(8,128)(2,1)S(1)}, u32[]{:S(2)}, u32[]{:S(2)}) async-start(bf16[256,16,256]{0,2,1:T(8,128)(2,1)} %bitcast.236), calls=%async_computation.2 | async-start | bytes 4194304 | tf_op jit(solution)/shard_map/all_to_all | solution.py:148
  19.3 8.1 %collective-permute-start = (bf16[256,128]{1,0:T(8,128)(2,1)S(1)}, bf16[256,128]{1,0:T(8,128)(2,1)S(1)}, u32[]{:S(2)}, u32[]{:S(2)}) collective-permute-start(bf16[256,128]{1,0:T(8,128)(2,1)S(1)} %broadcast_select_fusion.6), channel_id=1, source_target_pairs={{0,2},{2,0},{4,6},{6,4},{8,10},{10,8},{12,14},{14,12},{16,18},{18,... | collective-permute-start | bytes 196616 | tf_op jit(solution)/shard_map/ppermute | solution.py:110
  27.5 5.0 %collective-permute-start.1 = (bf16[512,128]{1,0:T(8,128)(2,1)S(1)}, bf16[512,128]{1,0:T(8,128)(2,1)S(1)}, u32[]{:S(2)}, u32[]{:S(2)}) collective-permute-start(bf16[512,128]{1,0:T(8,128)(2,1)S(1)} %maximum_select_fusion.3), channel_id=1, source_target_pairs={{0,4},{2,6},{4,0},{6,2},{8,12},{10,14},{12,8},{14,10},{16,20},{18,... | collective-permute-start | bytes 393224 | tf_op jit(solution)/shard_map/ppermute | solution.py:110
  32.6 25.8 %collective-permute-start.2 = (bf16[1024,128]{1,0:T(8,128)(2,1)S(1)}, bf16[1024,128]{1,0:T(8,128)(2,1)S(1)}, u32[]{:S(2)}, u32[]{:S(2)}) collective-permute-start(bf16[1024,128]{1,0:T(8,128)(2,1)S(1)} %maximum_select_fusion.2), channel_id=1, source_target_pairs={{0,8},{2,10},{4,12},{6,14},{8,0},{10,2},{12,4},{14,6},{16,24},{18,... | collective-permute-start | bytes 786440 | tf_op jit(solution)/shard_map/ppermute | solution.py:110
  58.5 5.3 %copy-start.15 = (bf16[2048,128]{1,0:T(8,128)(2,1)}, bf16[2048,128]{1,0:T(8,128)(2,1)S(1)}, u32[]{:S(2)}) copy-start(bf16[2048,128]{1,0:T(8,128)(2,1)S(1)} %maximum_select_fusion.1) | copy-start | bytes 1572868
  58.5 27.2 %collective-permute-start.3 = (bf16[2048,128]{1,0:T(8,128)(2,1)S(1)}, bf16[2048,128]{1,0:T(8,128)(2,1)}, u32[]{:S(2)}, u32[]{:S(2)}) collective-permute-start(bf16[2048,128]{1,0:T(8,128)(2,1)S(1)} %maximum_select_fusion.1), channel_id=1, source_target_pairs={{0,16},{2,18},{4,20},{6,22},{8,24},{10,26},{12,28},{14,30},{16,0},... | collective-permute-start | bytes 1572872 | tf_op jit(solution)/shard_map/ppermute | solution.py:110
  87.5 9.2 %copy-start.30 = (f32[64]{0:T(128)S(1)}, f32[64]{0:T(128)}, u32[]{:S(2)}) copy-start(f32[64]{0:T(128)} %param.12) | copy-start | bytes 772
  87.5 10.4 %copy-start.31 = (f32[64]{0:T(128)S(1)}, f32[64]{0:T(128)}, u32[]{:S(2)}) copy-start(f32[64]{0:T(128)} %param.11) | copy-start | bytes 772
  87.6 9.1 %copy-start.8 = (bf16[256,16,256]{0,2,1:T(8,128)(2,1)}, bf16[256,16,256]{0,2,1:T(8,128)(2,1)S(1)}, u32[]{:S(2)}) copy-start(bf16[256,16,256]{0,2,1:T(8,128)(2,1)S(1)} %all-to-all-done.2) | copy-start | bytes 6291460
  87.6 54.8 %all-to-all-start = ((bf16[256,16,256]{0,2,1:T(8,128)(2,1)}), bf16[256,16,256]{0,2,1:T(8,128)(2,1)}, u32[]{:S(2)}, u32[]{:S(2)}) async-start(bf16[256,16,256]{0,2,1:T(8,128)(2,1)} %bitcast.237), calls=%async_computation | async-start | bytes 4194304 | tf_op jit(solution)/shard_map/all_to_all | solution.py:151
  98.0 3.3 copy-start.26
  98.1 4.8 %collective-permute-start.4 = (bf16[4096,128]{1,0:T(8,128)(2,1)S(1)}, bf16[4096,128]{1,0:T(8,128)(2,1)S(1)}, u32[]{:S(2)}, u32[]{:S(2)}) collective-permute-start(bf16[4096,128]{1,0:T(8,128)(2,1)S(1)} %maximum_select_fusion), channel_id=1, source_target_pairs={{0,1},{1,0},{2,3},{3,2},{4,5},{5,4},{6,7},{7,6},{8,9},{9,8},{10,11... | collective-permute-start | bytes 3145736 | tf_op jit(solution)/shard_map/ppermute | solution.py:129
  101.5 49.1 %copy-start.20 = (f32[4,16,256]{2,1,0:T(8,128)}, f32[4,16,256]{2,1,0:T(8,128)S(1)}, u32[]{:S(2)}) copy-start(f32[4,16,256]{2,1,0:T(8,128)S(1)} %get-tuple-element.52) | copy-start | bytes 196612
  103.0 4.4 %copy-start.6 = (bf16[4096,128]{1,0:T(8,128)(2,1)}, bf16[4096,128]{1,0:T(8,128)(2,1)S(1)}, u32[]{:S(2)}) copy-start(bf16[4096,128]{1,0:T(8,128)(2,1)S(1)} %get-tuple-element.43) | copy-start | bytes 3145732
  104.7 2.7 copy-start.9
  156.5 2.0 copy-start.10
  158.5 4.0 %copy-start.2 = (bf16[4096,4,64]{0,2,1:T(8,128)(2,1)S(1)}, bf16[4096,4,64]{0,2,1:T(8,128)(2,1)}, u32[]{:S(2)}) copy-start(bf16[4096,4,64]{0,2,1:T(8,128)(2,1)} %reshape.149) | copy-start | bytes 6291460
  158.5 4.0 %copy-start.13 = (f32[16,256,256]{2,1,0:T(8,128)S(1)}, f32[16,256,256]{2,1,0:T(8,128)}, u32[]{:S(2)}) copy-start(f32[16,256,256]{2,1,0:T(8,128)} %fusion.113) | copy-start | bytes 12582916
  158.6 4.0 %copy-start.23 = (f32[1,4,16,256]{3,2,1,0:T(8,128)S(1)}, f32[1,4,16,256]{3,2,1,0:T(8,128)}, u32[]{:S(2)}) copy-start(f32[1,4,16,256]{3,2,1,0:T(8,128)} %copy.276) | copy-start | bytes 196612
  181.0 5.3 %copy-start = (f32[16,4,64,128]{3,2,1,0:T(8,128)}, f32[16,4,64,128]{3,2,1,0:T(8,128)S(1)}, u32[]{:S(2)}) copy-start(f32[16,4,64,128]{3,2,1,0:T(8,128)S(1)} %fusion.8) | copy-start | bytes 6291460
  181.0 5.3 %copy-start.24 = (f32[4,16]{1,0:T(4,128)S(1)}, f32[4,16]{1,0:T(4,128)}, u32[]{:S(2)}) copy-start(f32[4,16]{1,0:T(4,128)} %get-tuple-element.22) | copy-start | bytes 772
  186.2 2.0 copy-start.14
  186.2 2.0 copy-start.21
  195.5 3.7 %copy-start.5 = (f32[16,256,256]{2,1,0:T(8,128)S(1)}, f32[16,256,256]{2,1,0:T(8,128)}, u32[]{:S(2)}) copy-start(f32[16,256,256]{2,1,0:T(8,128)} %get-tuple-element.17) | copy-start | bytes 12582916
  195.5 3.7 %copy-start.7 = (bf16[4096,128]{1,0:T(8,128)(2,1)S(1)}, bf16[4096,128]{1,0:T(8,128)(2,1)}, u32[]{:S(2)}) copy-start(bf16[4096,128]{1,0:T(8,128)(2,1)} %copy-done.6) | copy-start | bytes 3145732
  195.6 4.4 %copy-start.12 = (f32[16,256,128,1]{2,1,3,0:T(8,128)S(1)}, f32[16,256,128,1]{2,1,3,0:T(8,128)}, u32[]{:S(2)}) copy-start(f32[16,256,128,1]{2,1,3,0:T(8,128)} %fusion.9) | copy-start | bytes 6291460
  200.0 7.0 %copy-start.3 = (bf16[4096,4,64]{0,2,1:T(8,128)(2,1)S(1)}, bf16[4096,4,64]{0,2,1:T(8,128)(2,1)}, u32[]{:S(2)}) copy-start(bf16[4096,4,64]{0,2,1:T(8,128)(2,1)} %reshape.149) | copy-start | bytes 6291460
  200.0 7.0 %copy-start.4 = (f32[16,4,64,256]{3,2,1,0:T(8,128)S(1)}, f32[16,4,64,256]{3,2,1,0:T(8,128)}, u32[]{:S(2)}) copy-start(f32[16,4,64,256]{3,2,1,0:T(8,128)} %get-tuple-element.56) | copy-start | bytes 12582916
  204.6 18.4 %collective-permute-start.20 = (f32[4096,128]{1,0:T(8,128)}, f32[4096,128]{1,0:T(8,128)}, u32[]{:S(2)}, u32[]{:S(2)}) collective-permute-start(f32[4096,128]{1,0:T(8,128)} %bitcast.65), channel_id=1, source_target_pairs={{0,1},{1,0},{2,3},{3,2},{4,5},{5,4},{6,7},{7,6},{8,9},{9,8},{10,11... | collective-permute-start | bytes 6291464 | tf_op jit(solution)/shard_map/ppermute | solution.py:169
  214.8 2.7 copy-start.1
  214.8 3.7 %copy-start.11 = (f32[4,16,64,128]{3,2,1,0:T(8,128)S(1)}, f32[4,16,64,128]{3,2,1,0:T(8,128)}, u32[]{:S(2)}) copy-start(f32[4,16,64,128]{3,2,1,0:T(8,128)} %copy-done.10) | copy-start | bytes 6291460
  218.6 3.7 %copy-start.25 = (f32[4,16]{1,0:T(4,128)S(1)}, f32[4,16]{1,0:T(4,128)}, u32[]{:S(2)}) copy-start(f32[4,16]{1,0:T(4,128)} %get-tuple-element.47) | copy-start | bytes 772
  218.6 3.7 %copy-start.32 = (f32[4,16]{1,0:T(4,128)S(1)}, f32[4,16]{1,0:T(4,128)}, u32[]{:S(2)}) copy-start(f32[4,16]{1,0:T(4,128)} %get-tuple-element.57) | copy-start | bytes 772
  218.6 4.0 %copy-start.18 = (f32[4,16,256]{2,1,0:T(8,128)S(1)}, f32[4,16,256]{2,1,0:T(8,128)}, u32[]{:S(2)}) copy-start(f32[4,16,256]{2,1,0:T(8,128)} %get-tuple-element.14) | copy-start | bytes 196612
  218.6 4.0 %copy-start.19 = (f32[4,16,256]{2,1,0:T(8,128)S(1)}, f32[4,16,256]{2,1,0:T(8,128)}, u32[]{:S(2)}) copy-start(f32[4,16,256]{2,1,0:T(8,128)} %get-tuple-element.15) | copy-start | bytes 196612
  218.6 4.0 %copy-start.22 = (f32[4,16,256]{2,1,0:T(8,128)S(1)}, f32[4,16,256]{2,1,0:T(8,128)}, u32[]{:S(2)}) copy-start(f32[4,16,256]{2,1,0:T(8,128)} %get-tuple-element.19) | copy-start | bytes 196612
  218.6 4.2 %copy-start.27 = (f32[4]{0:T(128)S(1)}, f32[4]{0:T(128)}, u32[]{:S(2)}) copy-start(f32[4]{0:T(128)} %copy-done.26) | copy-start | bytes 52
  227.0 6.1 %copy-start.28 = (f32[4]{0:T(128)S(1)}, f32[4]{0:T(128)}, u32[]{:S(2)}) copy-start(f32[4]{0:T(128)} %dynamic_slice.54) | copy-start | bytes 52
  227.0 101.7 %all-to-all-start.3 = ((f32[16,264,128]{2,1,0:T(8,128)}), f32[16,264,128]{2,1,0:T(8,128)}, u32[]{:S(2)}, u32[]{:S(2)}) async-start(f32[16,264,128]{2,1,0:T(8,128)} %pad_maximum_fusion), calls=%async_computation.3 | async-start | bytes 4325376 | tf_op jit(solution)/shard_map/all_to_all | solution.py:176
  236.6 9.2 %copy-start.29 = (s32[16]{0:T(128)S(1)}, s32[16]{0:T(128)}, u32[]{:S(2)}) copy-start(s32[16]{0:T(128)} %fusion.105) | copy-start | bytes 196
  244.6 11.8 %collective-permute-start.5 = (bf16[256,256]{1,0:T(8,128)(2,1)}, bf16[256,256]{1,0:T(8,128)(2,1)}, u32[]{:S(2)}, u32[]{:S(2)}) collective-permute-start(bf16[256,256]{1,0:T(8,128)(2,1)} %bitcast.21), channel_id=1, source_target_pairs={{0,2},{2,0},{4,6},{6,4},{8,10},{10,8},{12,14},{14,12},{16,18},{18,... | collective-permute-start | bytes 393224 | tf_op jit(solution)/shard_map/ppermute | solution.py:29
  248.6 10.5 %collective-permute-start.6 = (bf16[256,256]{1,0:T(8,128)(2,1)}, bf16[256,256]{1,0:T(8,128)(2,1)}, u32[]{:S(2)}, u32[]{:S(2)}) collective-permute-start(bf16[256,256]{1,0:T(8,128)(2,1)} %bitcast.262), channel_id=1, source_target_pairs={{0,4},{2,6},{4,0},{6,2},{8,12},{10,14},{12,8},{14,10},{16,20},{18,... | collective-permute-start | bytes 393224 | tf_op jit(solution)/shard_map/ppermute | solution.py:29
  250.6 16.3 %collective-permute-start.7 = (bf16[256,256]{1,0:T(8,128)(2,1)}, bf16[256,256]{1,0:T(8,128)(2,1)}, u32[]{:S(2)}, u32[]{:S(2)}) collective-permute-start(bf16[256,256]{1,0:T(8,128)(2,1)} %bitcast.261), channel_id=1, source_target_pairs={{0,6},{2,4},{4,2},{6,0},{8,14},{10,12},{12,10},{14,8},{16,22},{18,... | collective-permute-start | bytes 393224 | tf_op jit(solution)/shard_map/ppermute | solution.py:29
  251.7 21.3 %collective-permute-start.8 = (bf16[256,256]{1,0:T(8,128)(2,1)}, bf16[256,256]{1,0:T(8,128)(2,1)}, u32[]{:S(2)}, u32[]{:S(2)}) collective-permute-start(bf16[256,256]{1,0:T(8,128)(2,1)} %bitcast.27), channel_id=1, source_target_pairs={{0,8},{2,10},{4,12},{6,14},{8,0},{10,2},{12,4},{14,6},{16,24},{18,... | collective-permute-start | bytes 393224 | tf_op jit(solution)/shard_map/ppermute | solution.py:29
  251.8 24.1 %collective-permute-start.9 = (bf16[256,256]{1,0:T(8,128)(2,1)S(1)}, bf16[256,256]{1,0:T(8,128)(2,1)}, u32[]{:S(2)}, u32[]{:S(2)}) collective-permute-start(bf16[256,256]{1,0:T(8,128)(2,1)S(1)} %bitcast.260), channel_id=1, source_target_pairs={{0,10},{2,8},{4,14},{6,12},{8,2},{10,0},{12,6},{14,4},{16,26},{18,... | collective-permute-start | bytes 393224 | tf_op jit(solution)/shard_map/ppermute | solution.py:29
  256.4 24.0 %collective-permute-start.10 = (bf16[256,256]{1,0:T(8,128)(2,1)S(1)}, bf16[256,256]{1,0:T(8,128)(2,1)S(1)}, u32[]{:S(2)}, u32[]{:S(2)}) collective-permute-start(bf16[256,256]{1,0:T(8,128)(2,1)S(1)} %bitcast.259), channel_id=1, source_target_pairs={{0,12},{2,14},{4,8},{6,10},{8,4},{10,6},{12,0},{14,2},{16,28},{18,... | collective-permute-start | bytes 393224 | tf_op jit(solution)/shard_map/ppermute | solution.py:29
  259.2 26.2 %collective-permute-start.11 = (bf16[256,256]{1,0:T(8,128)(2,1)S(1)}, bf16[256,256]{1,0:T(8,128)(2,1)S(1)}, u32[]{:S(2)}, u32[]{:S(2)}) collective-permute-start(bf16[256,256]{1,0:T(8,128)(2,1)S(1)} %bitcast.258), channel_id=1, source_target_pairs={{0,14},{2,12},{4,10},{6,8},{8,6},{10,4},{12,2},{14,0},{16,30},{18,... | collective-permute-start | bytes 393224 | tf_op jit(solution)/shard_map/ppermute | solution.py:29
  266.9 31.3 %collective-permute-start.12 = (bf16[256,256]{1,0:T(8,128)(2,1)S(1)}, bf16[256,256]{1,0:T(8,128)(2,1)S(1)}, u32[]{:S(2)}, u32[]{:S(2)}) collective-permute-start(bf16[256,256]{1,0:T(8,128)(2,1)S(1)} %bitcast.257), channel_id=1, source_target_pairs={{0,16},{2,18},{4,20},{6,22},{8,24},{10,26},{12,28},{14,30},{16,0},... | collective-permute-start | bytes 393224 | tf_op jit(solution)/shard_map/ppermute | solution.py:29
  273.0 28.1 %collective-permute-start.13 = (bf16[256,256]{1,0:T(8,128)(2,1)S(1)}, bf16[256,256]{1,0:T(8,128)(2,1)S(1)}, u32[]{:S(2)}, u32[]{:S(2)}) collective-permute-start(bf16[256,256]{1,0:T(8,128)(2,1)S(1)} %bitcast.256), channel_id=1, source_target_pairs={{0,18},{2,16},{4,22},{6,20},{8,26},{10,24},{12,30},{14,28},{16,2},... | collective-permute-start | bytes 393224 | tf_op jit(solution)/shard_map/ppermute | solution.py:29
  276.0 29.6 %collective-permute-start.14 = (bf16[256,256]{1,0:T(8,128)(2,1)S(1)}, bf16[256,256]{1,0:T(8,128)(2,1)S(1)}, u32[]{:S(2)}, u32[]{:S(2)}) collective-permute-start(bf16[256,256]{1,0:T(8,128)(2,1)S(1)} %bitcast.255), channel_id=1, source_target_pairs={{0,20},{2,22},{4,16},{6,18},{8,28},{10,30},{12,24},{14,26},{16,4},... | collective-permute-start | bytes 393224 | tf_op jit(solution)/shard_map/ppermute | solution.py:29
  280.4 30.6 %collective-permute-start.15 = (bf16[256,256]{1,0:T(8,128)(2,1)S(1)}, bf16[256,256]{1,0:T(8,128)(2,1)S(1)}, u32[]{:S(2)}, u32[]{:S(2)}) collective-permute-start(bf16[256,256]{1,0:T(8,128)(2,1)S(1)} %bitcast.254), channel_id=1, source_target_pairs={{0,22},{2,20},{4,18},{6,16},{8,30},{10,28},{12,26},{14,24},{16,6},... | collective-permute-start | bytes 393224 | tf_op jit(solution)/shard_map/ppermute | solution.py:29
  285.4 33.9 %collective-permute-start.16 = (bf16[256,256]{1,0:T(8,128)(2,1)S(1)}, bf16[256,256]{1,0:T(8,128)(2,1)S(1)}, u32[]{:S(2)}, u32[]{:S(2)}) collective-permute-start(bf16[256,256]{1,0:T(8,128)(2,1)S(1)} %bitcast.253), channel_id=1, source_target_pairs={{0,24},{2,26},{4,28},{6,30},{8,16},{10,18},{12,20},{14,22},{16,8},... | collective-permute-start | bytes 393224 | tf_op jit(solution)/shard_map/ppermute | solution.py:29
  298.3 25.2 %collective-permute-start.17 = (bf16[256,256]{1,0:T(8,128)(2,1)S(1)}, bf16[256,256]{1,0:T(8,128)(2,1)S(1)}, u32[]{:S(2)}, u32[]{:S(2)}) collective-permute-start(bf16[256,256]{1,0:T(8,128)(2,1)S(1)} %bitcast.252), channel_id=1, source_target_pairs={{0,26},{2,24},{4,30},{6,28},{8,18},{10,16},{12,22},{14,20},{16,10}... | collective-permute-start | bytes 393224 | tf_op jit(solution)/shard_map/ppermute | solution.py:29
  301.1 27.0 %collective-permute-start.18 = (bf16[256,256]{1,0:T(8,128)(2,1)S(1)}, bf16[256,256]{1,0:T(8,128)(2,1)S(1)}, u32[]{:S(2)}, u32[]{:S(2)}) collective-permute-start(bf16[256,256]{1,0:T(8,128)(2,1)S(1)} %bitcast.251), channel_id=1, source_target_pairs={{0,28},{2,30},{4,24},{6,26},{8,20},{10,22},{12,16},{14,18},{16,12}... | collective-permute-start | bytes 393224 | tf_op jit(solution)/shard_map/ppermute | solution.py:29
  305.5 27.4 %collective-permute-start.19 = (bf16[256,256]{1,0:T(8,128)(2,1)S(1)}, bf16[256,256]{1,0:T(8,128)(2,1)S(1)}, u32[]{:S(2)}, u32[]{:S(2)}) collective-permute-start(bf16[256,256]{1,0:T(8,128)(2,1)S(1)} %bitcast.250), channel_id=1, source_target_pairs={{0,30},{2,28},{4,26},{6,24},{8,22},{10,20},{12,18},{14,16},{16,14}... | collective-permute-start | bytes 393224 | tf_op jit(solution)/shard_map/ppermute | solution.py:29
  330.4 13.4 %collective-permute-start.21 = (f32[256,128]{1,0:T(8,128)S(1)}, f32[256,128]{1,0:T(8,128)S(1)}, u32[]{:S(2)}, u32[]{:S(2)}) collective-permute-start(f32[256,128]{1,0:T(8,128)S(1)} %slice_reduce_fusion), channel_id=1, source_target_pairs={{0,1},{1,0},{2,3},{3,2},{4,5},{5,4},{6,7},{7,6},{8,9},{9,8},{10,11... | collective-permute-start | bytes 393224 | tf_op jit(solution)/shard_map/ppermute | solution.py:186
